TPU v7x, 512 devices: a whole 4x8x8 slice. The times are simulated.
512 devices in a mesh: fsdp: 64 (over y, x, core), tp: 8 (over z).
Axes of the slice: x: 4, y: 8, z: 8, core: 2. Of those that a mesh axis runs over, the one named last changes fastest.
Arguments:
- grads: bfloat16 [2, 12288, 2560], P(None, 'fsdp', 'tp'), may hold values from -16 to 16
- weights: float32 [2, 12288, 2560], P(None, 'fsdp', 'tp'), may hold values from -0.3 to 0.3
- basis: bfloat16 [2560, 2, 256], P('tp'), may hold values from -0.375 to 0.375
- first_moment: float32 [2, 12288, 256], P(None, 'fsdp', 'tp'), may hold values from -12 to 12
- second_moment: float32 [2, 12288, 256], P(None, 'fsdp', 'tp'), may hold values from 0.05 to 5
Outputs:
- weight_next: float32 [2, 12288, 2560], P(None, 'fsdp', 'tp')
- first_next: float32 [2, 12288, 256], P(None, 'fsdp', 'tp')
- second_next: float32 [2, 12288, 256], P(None, 'fsdp', 'tp')
- basis_next: bfloat16 [2560, 2, 256], P('tp')
All inputs are finite; a program needn't handle non-finite values.
Results may differ from a plain program's by a relative error of at most 0.0034.
Values may be sent and summed in bfloat16 or wider, within the bound.
No kernel may reach another device: no remote copies, remote signals or barrier semaphores. Data moves between devices by JAX's collectives and lax.ppermute only.
A program may use at most 64 MiB of HBM per device.

v0:
```python
import jax
import jax.numpy as jnp
from jax import lax
from jax.sharding import PartitionSpec as P

D = 2560
BETA_FIRST = 0.9
BETA_SECOND = 0.999
BIAS_FIRST = 0.9999734386011124
BIAS_SECOND = 0.0952078528862904
EPSILON = 1e-08
EPSILON_NORM = 1e-06
LEARNING_RATE = 0.1
GALORE_SCALE = 0.25


def adam_share(grad_share, first_moment, second_moment):
    first_next = BETA_FIRST * first_moment + (1.0 - BETA_FIRST) * grad_share
    second_next = BETA_SECOND * second_moment + (1.0 - BETA_SECOND) * grad_share * grad_share
    normal = first_next / BIAS_FIRST / (jnp.sqrt(second_next / BIAS_SECOND) + EPSILON)
    return (first_next, second_next, normal.astype(jnp.bfloat16))


def rebuild(image, sum_total, sum_cross):
    highest = lax.Precision.HIGHEST
    rank_width = image.shape[2]
    total = sum_total(jnp.sum(image * image, axis=(0, 2))) + EPSILON_NORM
    scaled = image * jnp.sqrt(rank_width / total)[None, :, None]
    cross = sum_cross(jnp.einsum("dmr,dms->mrs", scaled, scaled, precision=highest))
    shaped = 1.5 * scaled - 0.5 * jnp.einsum("dmr,mrs->dms", scaled, cross, precision=highest)
    return (jnp.sqrt(D / rank_width) * shaped).astype(jnp.bfloat16)


def shards(grads, weights, basis, first_moment, second_moment):
    projected_part = jnp.einsum("mfd,dmr->mfr", grads, basis, preferred_element_type=jnp.float32)
    summed_share = lax.psum_scatter(projected_part, "tp", scatter_dimension=2, tiled=True)
    first_next, second_next, normal_half = adam_share(summed_share, first_moment, second_moment)
    projected_half, normal_full = (
        lax.all_gather(summed_share.astype(jnp.bfloat16), "tp", axis=2, tiled=True),
        lax.all_gather(normal_half, "tp", axis=2, tiled=True),
    )
    update = jnp.einsum("mfr,dmr->mfd", normal_full, basis, preferred_element_type=jnp.float32)
    weight_next = weights - LEARNING_RATE * GALORE_SCALE * update

    def block_total(value):
        return lax.psum(value, "tp")

    def block_gram(value):
        return lax.psum(value, "tp")

    image = lax.psum(
        jnp.einsum("mfd,mfr->dmr", grads, projected_half, preferred_element_type=jnp.float32),
        "fsdp",
    )
    basis_next = rebuild(image, block_total, block_gram)
    return (weight_next, first_next, second_next, basis_next)


def solution(mesh):
    in_specs = (
        P(None, "fsdp", "tp"),
        P(None, "fsdp", "tp"),
        P("tp", None, None),
        P(None, "fsdp", "tp"),
        P(None, "fsdp", "tp"),
    )
    out_specs = (
        P(None, "fsdp", "tp"),
        P(None, "fsdp", "tp"),
        P(None, "fsdp", "tp"),
        P("tp", None, None),
    )
    return jax.shard_map(shards, mesh=mesh, in_specs=in_specs, out_specs=out_specs, check_vma=False)
```

profile of v0, /device:TPU:2, one launch (start us, length us, event | category | flops | bytes accessed | tf_op | source)
XLA Modules:
  0.0 383.9 jit_solution(17990277985158223660)
XLA Ops:
  7.2 0.0 copy-start
  7.2 0.0 reduce-scatter.2.cloned.1.call-start
  7.2 0.9 copy-done
  8.1 2.1 fusion.11
  10.2 0.0 reduce-scatter.2.cloned.1.call-update
  10.3 0.0 copy-start.2
  10.3 0.0 all-reduce.3.cloned.1.call-start
  10.3 46.8 %reduce-scatter.2.cloned.1.call-done = f32[2,192,32]{1,2,0:T(8,128)} async-done(((f32[2,192,256]{1,2,0:T(8,128)}), f32[2,192,32]{1,2,0:T(8,128)}) %reduce-scatter.2.cloned.1.call-update) | async-done | bytes 49168 | tf_op jit(solution)/shard_map/reduce_scatter | solution.py:36
  57.2 0.0 copy-done.4
  57.2 1.6 divide_convert_fusion
  58.8 24.8 %all_gather.7 = bf16[2,192,256]{1,2,0:T(8,128)(2,1)S(1)} all-gather(bf16[2,192,32]{1,2,0:T(8,128)(2,1)S(1)} %get-tuple-element.11), channel_id=1, replica_groups=mesh['fsdp'=64,'tp'=8] {'tp'}, dimensions={2}, use_global_device_ids=true | all-gather | bytes 221184 | tf_op jit(solution)/shard_map/all_gather | solution.py:39
  83.6 1.2 convolution_bitcast_fusion
  84.7 0.0 all-reduce.3.cloned.1.call-update
  84.8 0.0 all-reduce.5.cloned.1.call-start
  84.8 192.2 %all-reduce.3.cloned.1.call-done = f32[320,2,256]{2,0,1:T(8,128)} async-done(((f32[320,2,256]{2,0,1:T(8,128)}), f32[320,2,256]{2,0,1:T(8,128)}) %all-reduce.3.cloned.1.call-update) | async-done | bytes 655376 | tf_op jit(solution)/shard_map/psum | solution.py:51
  277.0 1.3 multiply_reduce_fusion
  278.3 18.1 %psum.22 = f32[2]{0:T(128)S(1)} all-reduce(f32[2]{0:T(128)S(1)} %multiply_reduce_fusion), channel_id=1, replica_groups=mesh['fsdp'=64,'tp'=8] {'tp'}, use_global_device_ids=true, to_apply=%region_3.0 | all-reduce | flops 2 | bytes 16 | tf_op jit(solution)/shard_map/psum | solution.py:46
  296.4 2.4 fusion.5
  298.8 0.0 all-reduce.5.cloned.1.call-update
  298.8 25.0 %all_gather.6 = bf16[2,192,256]{1,2,0:T(8,128)(2,1)S(1)} all-gather(bf16[2,192,32]{1,2,0:T(8,128)(2,1)S(1)} %get-tuple-element.8), channel_id=1, replica_groups=mesh['fsdp'=64,'tp'=8] {'tp'}, dimensions={2}, use_global_device_ids=true | all-gather | bytes 221184 | tf_op jit(solution)/shard_map/all_gather | solution.py:40
  323.9 1.2 fusion.3
  325.0 49.4 %all-reduce.5.cloned.1.call-done = f32[2,256,256]{2,1,0:T(8,128)} async-done(((f32[2,256,256]{2,1,0:T(8,128)}), f32[2,256,256]{2,1,0:T(8,128)}) %all-reduce.5.cloned.1.call-update) | async-done | bytes 524304 | tf_op jit(solution)/shard_map/psum | solution.py:49
  374.4 1.9 fusion.4
  376.3 1.1 copy.11
  (9 shorter events, 0.0 us)
Async XLA Ops:
  7.2 1.0 copy-start
  7.2 50.0 %reduce-scatter.2.cloned.1.call-start = ((), (), s32[]{:S(2)}) async-start(), calls=%async_computation.1 | async-start | bytes 589824 | tf_op jit(solution)/shard_map/reduce_scatter | solution.py:36
  10.2 46.9 %copy-start.4 = (f32[2,192,32]{1,2,0:T(8,128)S(1)}, f32[2,192,32]{1,2,0:T(8,128)}, u32[]{:S(2)}) copy-start(f32[2,192,32]{1,2,0:T(8,128)} %param.8) | copy-start | bytes 147460
  10.2 46.9 %copy-start.5 = (f32[2,192,32]{1,2,0:T(8,128)S(1)}, f32[2,192,32]{1,2,0:T(8,128)}, u32[]{:S(2)}) copy-start(f32[2,192,32]{1,2,0:T(8,128)} %param.9) | copy-start | bytes 147460
  10.3 73.3 %copy-start.2 = (bf16[2,192,320]{2,1,0:T(8,128)(2,1)S(1)}, bf16[2,192,320]{2,1,0:T(8,128)(2,1)}, u32[]{:S(2)}) copy-start(bf16[2,192,320]{2,1,0:T(8,128)(2,1)} %param.5) | copy-start | bytes 737284
  10.3 266.7 %all-reduce.3.cloned.1.call-start = ((), (), s32[]{:S(2)}) async-start(), calls=%async_computation.2 | async-start | bytes 1310720 | tf_op jit(solution)/shard_map/psum | solution.py:51
  84.8 289.6 %all-reduce.5.cloned.1.call-start = ((), (), s32[]{:S(2)}) async-start(), calls=%async_computation.3 | async-start | bytes 1048576 | tf_op jit(solution)/shard_map/psum | solution.py:49
  277.0 19.4 %copy-start.1 = (f32[320,2,256]{2,0,1:T(8,128)S(1)}, f32[320,2,256]{2,0,1:T(8,128)}, u32[]{:S(2)}) copy-start(f32[320,2,256]{2,0,1:T(8,128)} %all-reduce.3.cloned.1.call-done) | copy-start | bytes 1966084
  298.8 25.0 %copy-start.3 = (f32[2,192,320]{2,1,0:T(8,128)S(1)}, f32[2,192,320]{2,1,0:T(8,128)}, u32[]{:S(2)}) copy-start(f32[2,192,320]{2,1,0:T(8,128)} %param.6) | copy-start | bytes 1474564
Sparse Core Ops, SparseCore 0:
  11.4 45.7 reduce-scatter.1
  84.9 192.0 all-reduce.2
  299.0 75.3 all-reduce.4
where the time goes:
time: 384 us
  waiting for transfers between devices  288 us (75%)
  blocking collectives  67.9 us (18%)
  between operations  13.8 us (4%)
  matrix products  8.7 us (2%)
    psum x1, waiting for transfers between devices, shards(): lax.psum(jnp.einsum('mfd,mfr->dmr', grads, projected_half, preferred_elem...  192 us
    psum x1, waiting for transfers between devices, block_gram(): return lax.psum(value, 'tp')  49.4 us
    reduce_scatter x1, waiting for transfers between devices, shards(): lax.psum_scatter(projected_part, 'tp', scatter_dimension=2, tiled=True)  46.8 us
    all_gather x1, blocking collectives, shards(): lax.all_gather(normal_half, 'tp', axis=2, tiled=True)  25 us
    all_gather x1, blocking collectives, shards(): lax.all_gather(summed_share.astype(jnp.bfloat16), 'tp', axis=2, tiled=True)  24.8 us
    psum x1, blocking collectives, block_total(): return lax.psum(value, 'tp')  18.1 us
  transfers between devices with their start and end apart: 3, of which 3 were waited for; matrix products, arithmetic and copies ran while one was open for 0% of the time, Pallas kernels for 0%

commit v1 on v0

--- a/solution.py
+++ b/solution.py
@@ -48,10 +48,8 @@
     def block_gram(value):
         return lax.psum(value, "tp")
 
-    image = lax.psum(
-        jnp.einsum("mfd,mfr->dmr", grads, projected_half, preferred_element_type=jnp.float32),
-        "fsdp",
-    )
+    packet = jnp.einsum("mfd,mfr->dmr", grads, projected_half, preferred_element_type=jnp.float32)
+    image = jnp.sum(lax.all_gather(packet, "fsdp"), 0)
     basis_next = rebuild(image, block_total, block_gram)
     return (weight_next, first_next, second_next, basis_next)
 

time: 384 us -> 372 us (0.969)
  waiting for transfers between devices: 288 us -> 262 us
  other arithmetic: 2.95 us -> 16.4 us
    psum x1 -> x0, waiting for transfers between devices: 192 us -> none  [shards(): lax.psum(jnp.einsum('mfd,mfr->dmr', grads, projected_half, preferred_elem...]
    all_gather x0 -> x1, waiting for transfers between devices: none -> 165 us  [shards(): image = jnp.sum(lax.all_gather(packet, 'fsdp'), 0)]
    reduce_sum x0 -> x1, other arithmetic: none -> 14.6 us  [shards(): image = jnp.sum(lax.all_gather(packet, 'fsdp'), 0)]
where the time goes in v1:
time: 372 us
  waiting for transfers between devices  262 us (70%)
  blocking collectives  67.9 us (18%)
  other arithmetic  16.4 us (4%)
  between operations  13.8 us (4%)
  matrix products  9.7 us (3%)
    all_gather x1, waiting for transfers between devices, shards(): image = jnp.sum(lax.all_gather(packet, 'fsdp'), 0)  165 us
    psum x1, waiting for transfers between devices, block_gram(): return lax.psum(value, 'tp')  49.5 us
    reduce_scatter x1, waiting for transfers between devices, shards(): lax.psum_scatter(projected_part, 'tp', scatter_dimension=2, tiled=True)  46.9 us
    all_gather x1, blocking collectives, shards(): lax.all_gather(normal_half, 'tp', axis=2, tiled=True)  25 us
    all_gather x1, blocking collectives, shards(): lax.all_gather(summed_share.astype(jnp.bfloat16), 'tp', axis=2, tiled=True)  24.8 us
    psum x1, blocking collectives, block_total(): return lax.psum(value, 'tp')  18.1 us
    reduce_sum x1, other arithmetic, shards(): image = jnp.sum(lax.all_gather(packet, 'fsdp'), 0)  14.6 us
  transfers between devices with their start and end apart: 3, of which 3 were waited for; matrix products, arithmetic and copies ran while one was open for 0% of the time, Pallas kernels for 0%

profile of v1, /device:TPU:2, one launch (start us, length us, event | category | flops | bytes accessed | tf_op | source)
XLA Modules:
  0.0 371.5 jit_solution(6253818184470670349)
XLA Ops:
  7.2 0.0 copy-start
  7.2 0.0 copy-start.1
  7.2 0.0 reduce-scatter.2.cloned.1.call-start
  7.2 0.9 copy-done
  8.1 2.1 fusion.11
  10.2 0.0 reduce-scatter.2.cloned.1.call-update
  10.3 0.0 all-gather.3.cloned.1.call-start
  10.3 46.9 %reduce-scatter.2.cloned.1.call-done = f32[2,192,32]{1,2,0:T(8,128)} async-done(((f32[2,192,256]{1,2,0:T(8,128)}), f32[2,192,32]{1,2,0:T(8,128)}) %reduce-scatter.2.cloned.1.call-update) | async-done | bytes 49168 | tf_op jit(solution)/shard_map/reduce_scatter | solution.py:36
  57.2 1.6 divide_convert_fusion
  58.8 24.8 %all_gather.13 = bf16[2,192,256]{1,2,0:T(8,128)(2,1)S(1)} all-gather(bf16[2,192,32]{1,2,0:T(8,128)(2,1)S(1)} %get-tuple-element.11), channel_id=1, replica_groups=mesh['fsdp'=64,'tp'=8] {'tp'}, dimensions={2}, use_global_device_ids=true | all-gather | bytes 221184 | tf_op jit(solution)/shard_map/all_gather | solution.py:39
  83.6 2.1 convolution_bitcast_fusion
  85.7 0.0 all-gather.3.cloned.1.call-update
  85.8 0.0 all-reduce.2.cloned.1.call-start
  85.8 165.2 %all-gather.3.cloned.1.call-done = f32[20480,2,256]{2,0,1:T(8,128)} async-done(((f32[320,2,256]{2,0,1:T(8,128)}), f32[20480,2,256]{2,0,1:T(8,128)}) %all-gather.3.cloned.1.call-update) | async-done | bytes 41943056 | tf_op jit(solution)/shard_map/all_gather | solution.py:52
  251.0 14.6 %reduce_sum.18 = f32[320,2,256]{2,0,1:T(8,128)S(1)} reduce(f32[64,320,2,256]{3,1,0,2:T(8,128)} %bitcast.16, f32[]{:T(128)} %constant.10.clone.1), dimensions={0}, to_apply=%region_1.0 | reduce | flops 10321920 | bytes 42598404 | tf_op jit(solution)/shard_map/reduce_sum | solution.py:52
  265.6 0.2 multiply_reduce_fusion
  265.8 18.1 %psum.14 = f32[2]{0:T(128)S(1)} all-reduce(f32[2]{0:T(128)S(1)} %multiply_reduce_fusion), channel_id=1, replica_groups=mesh['fsdp'=64,'tp'=8] {'tp'}, use_global_device_ids=true, to_apply=%region_3.0 | all-reduce | flops 2 | bytes 16 | tf_op jit(solution)/shard_map/psum | solution.py:46
  283.9 2.4 fusion.5
  286.3 0.0 all-reduce.2.cloned.1.call-update
  286.4 25.0 %all_gather.12 = bf16[2,192,256]{1,2,0:T(8,128)(2,1)S(1)} all-gather(bf16[2,192,32]{1,2,0:T(8,128)(2,1)S(1)} %get-tuple-element.8), channel_id=1, replica_groups=mesh['fsdp'=64,'tp'=8] {'tp'}, dimensions={2}, use_global_device_ids=true | all-gather | bytes 221184 | tf_op jit(solution)/shard_map/all_gather | solution.py:40
  311.4 1.2 fusion.3
  312.6 49.5 %all-reduce.2.cloned.1.call-done = f32[2,256,256]{2,1,0:T(8,128)} async-done(((f32[2,256,256]{2,1,0:T(8,128)}), f32[2,256,256]{2,1,0:T(8,128)}) %all-reduce.2.cloned.1.call-update) | async-done | bytes 524304 | tf_op jit(solution)/shard_map/psum | solution.py:49
  362.0 1.9 fusion.4
  363.9 1.1 copy.11
  (2 shorter events, 0.0 us)
Async XLA Ops:
  7.2 1.0 copy-start
  7.2 304.2 %copy-start.1 = (f32[2,192,320]{2,1,0:T(8,128)S(1)}, f32[2,192,320]{2,1,0:T(8,128)}, u32[]{:S(2)}) copy-start(f32[2,192,320]{2,1,0:T(8,128)} %param.6) | copy-start | bytes 1474564
  7.2 50.0 %reduce-scatter.2.cloned.1.call-start = ((), (), s32[]{:S(2)}) async-start(), calls=%async_computation.1 | async-start | bytes 589824 | tf_op jit(solution)/shard_map/reduce_scatter | solution.py:36
  10.3 240.8 %all-gather.3.cloned.1.call-start = ((), (), s32[]{:S(2)}) async-start(), calls=%async_computation.3 | async-start | bytes 42598400 | tf_op jit(solution)/shard_map/all_gather | solution.py:52
  85.8 276.3 %all-reduce.2.cloned.1.call-start = ((), (), s32[]{:S(2)}) async-start(), calls=%async_computation.2 | async-start | bytes 1048576 | tf_op jit(solution)/shard_map/psum | solution.py:49
Sparse Core Ops, SparseCore 0:
  11.4 45.7 reduce-scatter.1
  85.9 165.1 all-gather.2
  286.5 75.4 all-reduce.1
